TPU v7x, 256 devices: a whole 4x4x8 slice. The times are simulated.
256 devices in a mesh: section: 2 (over core), tok: 32 (over z, y), rep: 4 (over x).
Axes of the slice: x: 4, y: 4, z: 8, core: 2. Of those that a mesh axis runs over, the one named last changes fastest.
Arguments:
- inputs: bfloat16 [2, 4096, 1024], P(None, 'tok')
- segment_ids: int32 [2, 4096], replicated, may hold values from 0 to 7, as said below
- picks: int32 [2, 4096, 2], P(None, 'tok'), may hold values from 0 to 15, all different within a row; in each aligned block of 128 rows (0 to 127, 128 to 255, ..., all dimensions but the last counted through in order) at most 20 rows name the same one
- page_table: int32 [2, 32], replicated, may hold values from 0 to 31, each once within a row
- norm_gains: float32 [2, 2, 1024], P('section'), may hold values from 0.1 to 1.9
- attn_qkv: bfloat16 [2, 1024, 3, 1024], P('section', None, None, 'rep')
- attn_out: bfloat16 [2, 1024, 1024], P('section', 'rep'), may hold values from -0.1875 to 0.1875
- router: bfloat16 [2, 1024, 16], P('section')
- expert_in: bfloat16 [2, 32, 1024, 2, 1408], P('section', 'tok', None, None, 'rep'), may hold values from -0.1875 to 0.1875
- expert_out: bfloat16 [2, 32, 1408, 1024], P('section', 'tok', 'rep')
Outputs:
- layer_out: bfloat16 [2, 2, 4096, 1024], P('section', None, 'tok')
- kv_pages: bfloat16 [2, 2, 32, 128, 2, 1024], P('section', None, 'tok', None, None, 'rep')
Inputs may be any that keep to these rules, and one draw needn't show every extreme that they name: `picks`: within the tokens of one index of tok in one micro-batch, at most 20 tokens pick one expert, and some expert is picked by exactly 20. `segment_ids`: ids never fall along a micro-batch; every prompt has at least one token, a prompt spans at most 2048 tokens and one spans exactly 2048. `page_table`: each row is a permutation.
All inputs are finite; a program needn't handle non-finite values.
Results may differ from a plain program's by a relative error of at most 0.034.
Values may be sent and summed in bfloat16 or wider, within the bound.
No kernel may reach another device: no remote copies, remote signals or barrier semaphores. Data moves between devices by JAX's collectives and lax.ppermute only.
A program may use at most 128 MiB of HBM per device.

v0:
```python
import jax
import jax.numpy as jnp
from jax import lax
from jax.sharding import PartitionSpec as P

HEAD_DIM = 64
TOP = 2
PAGE = 128
CAP = 20
NEG_FILL = -1e30


def shifted(value, axis, steps):
    count = lax.axis_size(axis)
    first, last = (max(0, -steps), min(count, count - steps))
    return lax.ppermute(value, axis, [(source, source + steps) for source in range(first, last)])


def rms_scale(values, gains):
    return values * lax.rsqrt(jnp.mean(values * values, axis=-1, keepdims=True) + 1e-06) * gains


def attend(carry, queries, keys_vals, seg_query, pos_query, seg_key, pos_key):
    run_max, run_sum, run_acc = carry
    heads_here = run_acc.shape[0]
    head_size = run_acc.shape[2]
    rows_key = keys_vals.shape[0]
    key_part = keys_vals[:, 0].reshape(rows_key, heads_here, head_size)
    val_part = keys_vals[:, 1].reshape(rows_key, heads_here, head_size).astype(jnp.float32)
    scores = jnp.einsum(
        "thd,nhd->htn", queries, key_part, preferred_element_type=jnp.float32
    ) * head_size ** (-0.5)
    visible = (seg_query[:, None] == seg_key[None, :]) & (pos_query[:, None] >= pos_key[None, :])
    masked = jnp.where(visible[None], scores, NEG_FILL)
    new_max = jnp.maximum(run_max, jnp.max(masked, axis=-1))
    weights = jnp.where(visible[None], jnp.exp(masked - new_max[..., None]), 0.0)
    decay = jnp.exp(run_max - new_max)
    run_sum = run_sum * decay + jnp.sum(weights, axis=-1)
    run_acc = run_acc * decay[..., None] + jnp.einsum(
        "htn,nhd->htd", weights, val_part, precision=lax.Precision.HIGHEST
    )
    return (new_max, run_sum, run_acc)


def place_pages(pages, keys_vals, table_row, tok_index):
    rows_here = keys_vals.shape[0]
    blocks_dev = pages.shape[0]
    page_rows = pages.shape[1]
    block_ids = jnp.arange(table_row.shape[0], dtype=jnp.int32)
    wanted = tok_index * blocks_dev + 0
    source = jnp.sum(jnp.where(table_row == wanted, block_ids, 0))
    offset = source * page_rows
    inside = (offset >= 0) & (offset + page_rows <= rows_here)
    block = lax.dynamic_slice_in_dim(
        keys_vals, jnp.clip(offset, 0, rows_here - page_rows), page_rows, 0
    )
    updated = [jnp.where(inside, block, pages[0])]
    return jnp.stack(updated)


def per_device(
    inputs,
    segment_ids,
    picks,
    page_table,
    norm_gains,
    attn_qkv,
    attn_out,
    router,
    expert_in,
    expert_out,
):
    section_index = lax.axis_index("section")
    tok_index = lax.axis_index("tok")
    tok_count = lax.axis_size("tok")
    micro_count = inputs.shape[0]
    tok_rows = inputs.shape[1]
    width = inputs.shape[2]
    col_width = attn_qkv.shape[3]
    head_count = col_width // HEAD_DIM
    experts_all = router.shape[2]
    local_pieces = expert_in.shape[1]
    split_count = local_pieces * tok_count // experts_all
    blocks_dev = tok_rows // PAGE
    row_ids = jnp.arange(tok_rows, dtype=jnp.int32)
    pos_query = tok_index * tok_rows + row_ids
    gains = norm_gains[0]
    w_qkv = attn_qkv[0].reshape(width, 3 * col_width)
    w_out = attn_out[0]
    w_router = router[0]
    w_in = expert_in[0]
    w_down = expert_out[0]
    outputs = [jnp.zeros((tok_rows, width), jnp.bfloat16) for slot_micro in range(micro_count)]
    page_out = [
        jnp.zeros((blocks_dev, PAGE, 2, col_width), jnp.bfloat16)
        for slot_micro in range(micro_count)
    ]
    received = jnp.zeros((tok_rows, width), jnp.bfloat16)
    for round_index in range(micro_count + 1):
        own_micro = round_index - section_index
        micro_index = jnp.clip(own_micro, 0, micro_count - 1)
        fresh = inputs[min(round_index, micro_count - 1)]
        layer_in = jnp.where(section_index == 0, fresh, received)
        seg_all = lax.dynamic_index_in_dim(segment_ids, micro_index, 0, keepdims=False)
        seg_query = lax.dynamic_slice_in_dim(seg_all, tok_index * tok_rows, tok_rows)
        table_row = lax.dynamic_index_in_dim(page_table, micro_index, 0, keepdims=False)
        pick_rows = lax.dynamic_index_in_dim(picks, micro_index, 0, keepdims=False)
        resid = layer_in.astype(jnp.float32)
        normed = rms_scale(resid, gains[0]).astype(jnp.bfloat16)
        projected = jnp.dot(normed, w_qkv, preferred_element_type=jnp.float32).astype(jnp.bfloat16)
        projected = projected.reshape(tok_rows, 3, col_width)
        queries = projected[:, 0].reshape(tok_rows, head_count, HEAD_DIM)
        keys_vals = projected[:, 1:]
        soft_init = (
            jnp.full((head_count, tok_rows), NEG_FILL, jnp.float32),
            jnp.zeros((head_count, tok_rows), jnp.float32),
            jnp.zeros((head_count, tok_rows, HEAD_DIM), jnp.float32),
        )
        empty_pages = jnp.zeros((blocks_dev, PAGE, 2, col_width), jnp.bfloat16)
        piece = lax.all_gather(keys_vals, "tok", axis=0, tiled=True)
        rows_key = piece.shape[0]
        step_rows = 1024
        while rows_key % step_rows != 0:
            step_rows = step_rows // 2
        turns = rows_key // step_rows

        def key_block(index, soft_now):
            start = index * step_rows
            block = lax.dynamic_slice_in_dim(piece, start, step_rows, 0)
            seg_key = lax.dynamic_slice_in_dim(seg_all, start, step_rows)
            pos_key = start + jnp.arange(step_rows, dtype=jnp.int32)
            return attend(soft_now, queries, block, seg_query, pos_query, seg_key, pos_key)

        soft_next = lax.fori_loop(0, turns, key_block, soft_init)
        pages = place_pages(empty_pages, piece, table_row, tok_index)
        run_max, run_sum, run_acc = soft_next
        context = (
            (run_acc / run_sum[..., None])
            .transpose(1, 0, 2)
            .reshape(tok_rows, col_width)
            .astype(jnp.bfloat16)
        )
        attn_part = jnp.dot(context, w_out, preferred_element_type=jnp.float32)
        mid = resid + lax.psum(attn_part, "rep")
        normed_mid = rms_scale(mid, gains[1]).astype(jnp.bfloat16)
        logits = jnp.dot(normed_mid, w_router, preferred_element_type=jnp.float32)
        expert_ids = jnp.arange(experts_all, dtype=jnp.int32)
        chosen = (pick_rows[:, :, None] == expert_ids[None, None, :]).astype(jnp.int32)
        picked_logit = jnp.sum(chosen.astype(jnp.float32) * logits[:, None, :], axis=-1)
        top_logit = jnp.max(picked_logit, axis=-1, keepdims=True)
        raised = jnp.exp(picked_logit - top_logit)
        gate_vals = raised / jnp.sum(raised, axis=-1, keepdims=True)
        ordered = chosen.transpose(1, 0, 2).reshape(TOP * tok_rows, experts_all)
        slot_of = jnp.sum((jnp.cumsum(ordered, axis=0) - 1) * ordered, axis=-1)
        flat_slot = pick_rows.T.reshape(TOP * tok_rows) * CAP + slot_of
        slot_ids = jnp.arange(experts_all * CAP, dtype=jnp.int32)
        hits = (flat_slot[:, None] == slot_ids[None, :]).astype(jnp.int32)
        hits = jnp.sum(hits.reshape(TOP, tok_rows, experts_all * CAP), axis=0).astype(jnp.bfloat16)
        dispatch = lax.dot_general(
            hits, normed_mid, (((0,), (0,)), ((), ())), preferred_element_type=jnp.float32
        ).astype(jnp.bfloat16)
        copies = jnp.broadcast_to(
            dispatch.reshape(experts_all, 1, CAP, width), (experts_all, split_count, CAP, width)
        )
        copies = copies.reshape(tok_count, local_pieces, CAP, width)
        act = jnp.einsum(
            "secd,edgf->secgf",
            lax.all_to_all(copies, "tok", split_axis=0, concat_axis=0, tiled=True),
            w_in,
            preferred_element_type=jnp.float32,
        )
        hidden = (jax.nn.gelu(act[..., 0, :]) * act[..., 1, :]).astype(jnp.bfloat16)
        returned = lax.all_to_all(
            jnp.einsum("secf,efd->secd", hidden, w_down, preferred_element_type=jnp.float32).astype(
                jnp.bfloat16
            ),
            "tok",
            split_axis=0,
            concat_axis=0,
            tiled=True,
        )
        summed = jnp.sum(
            returned.reshape(experts_all, split_count, CAP, width).astype(jnp.float32), axis=1
        )
        summed = summed.reshape(experts_all * CAP, width)
        gathered = jnp.take(summed, flat_slot, axis=0).reshape(TOP, tok_rows, width)
        expert_local = jnp.sum(gate_vals.T[:, :, None] * gathered, axis=0)
        expert_total = lax.psum(expert_local, "rep")
        layer_result = (mid + expert_total).astype(jnp.bfloat16)
        for slot_micro in range(micro_count):
            if slot_micro == round_index or slot_micro == round_index - 1:
                taken = own_micro == slot_micro
                outputs[slot_micro] = jnp.where(taken, layer_result, outputs[slot_micro])
                page_out[slot_micro] = jnp.where(taken, pages, page_out[slot_micro])
        if round_index < micro_count:
            received = shifted(layer_result, "section", 1)
    return (jnp.stack(outputs)[None], jnp.stack(page_out)[None])


def solution(mesh):
    return jax.shard_map(
        per_device,
        mesh=mesh,
        in_specs=(
            P(None, "tok", None),
            P(),
            P(None, "tok", None),
            P(),
            P("section", None, None),
            P("section", None, None, "rep"),
            P("section", "rep", None),
            P("section", None, None),
            P("section", "tok", None, None, "rep"),
            P("section", "tok", "rep", None),
        ),
        out_specs=(P("section", None, "tok", None), P("section", None, "tok", None, None, "rep")),
        check_vma=False,
    )
```

profile of v0, /device:TPU:8, one launch (start us, length us, event | category | flops | bytes accessed | tf_op | source)
XLA Modules:
  0.0 1003.8 jit_solution(15672951469307340651)
XLA Ops:
  20.4 79.9 %all-gather.4.cloned.1.call-done = bf16[4096,2,256]{0,2,1:T(8,128)(2,1)} async-done(((bf16[128,2,256]{0,2,1:T(8,128)(2,1)}), bf16[4096,2,256]{0,2,1:T(8,128)(2,1)}) %all-gather.4.cloned.1.call-update) | async-done | bytes 4194320 | tf_op jit(solution)/shard_map/all_gather | solution.py:120
  100.3 34.9 %while.54 = (s32[]{:T(128)}, f32[4,128]{1,0:T(4,128)S(1)}, f32[4,128]{1,0:T(4,128)S(1)}, f32[4,128,64]{1,2,0:T(8,128)}, s32[128]{0:T(128)}, /*index=5*/s32[4096]...) while((s32[]{:T(128)}, f32[4,128]{1,0:T(4,128)S(1)}, ...), condition=%wide.region_4.5_spmd.clone, body=%wide.region_1.4_spmd.clone.sunk | while | flops 476548736 | bytes 14800775 | solution.py:134
  102.7 2.1 constant_dynamic-slice_fusion.18
  111.4 2.1 constant_dynamic-slice_fusion.18
  120.1 2.1 constant_dynamic-slice_fusion.18
  128.9 2.1 constant_dynamic-slice_fusion.18
  140.8 46.1 %all-reduce.7.cloned.1.call-done = f32[128,1024]{1,0:T(8,128)} async-done(((f32[128,1024]{1,0:T(8,128)}), f32[128,1024]{1,0:T(8,128)}) %all-reduce.7.cloned.1.call-update) | async-done | bytes 524304 | tf_op jit(solution)/shard_map/psum | solution.py:144
  190.6 47.1 %all_to_all.30 = bf16[32,1,20,1024]{3,2,1,0:T(8,128)(2,1)S(1)} all-to-all(bf16[32,1,20,1024]{3,2,1,0:T(8,128)(2,1)S(1)} %bitcast.386), channel_id=1, replica_groups=mesh['section'=2,'tok'=32,'rep'=4] {'tok'}, dimensions={0} | all-to-all | bytes 2621440 | tf_op jit(solution)/shard_map/all_to_all | solution.py:168
  242.3 5.7 all-to-all-start.1
  251.2 33.0 %all-to-all-done.1 = bf16[32,1,20,1024]{3,2,1,0:T(8,128)(2,1)S(1)} async-done(((bf16[32,1,20,1024]{3,2,1,0:T(8,128)(2,1)}), bf16[32,1,20,1024]{3,2,1,0:T(8,128)(2,1)S(1)}, u32[]{:S(2)}, u32[]{:S(2)}) %all-to-all-start.1) | async-done | bytes 1310752 | tf_op jit(solution)/shard_map/all_to_all | solution.py:173
  287.2 2.2 gather_fusion
  291.7 45.9 %all-reduce.9.cloned.1.call-done = f32[128,1024]{1,0:T(8,128)} async-done(((f32[128,1024]{1,0:T(8,128)}), f32[128,1024]{1,0:T(8,128)}) %all-reduce.9.cloned.1.call-update) | async-done | bytes 524304 | tf_op jit(solution)/shard_map/psum | solution.py:188
  348.5 79.2 %all-gather.6.cloned.1.call-done = bf16[4096,2,256]{0,2,1:T(8,128)(2,1)} async-done(((bf16[128,2,256]{0,2,1:T(8,128)(2,1)}), bf16[4096,2,256]{0,2,1:T(8,128)(2,1)}) %all-gather.6.cloned.1.call-update) | async-done | bytes 4194320 | tf_op jit(solution)/shard_map/all_gather | solution.py:120
  427.7 35.0 %while.55 = (s32[]{:T(128)}, f32[4,128]{1,0:T(4,128)S(1)}, f32[4,128]{1,0:T(4,128)S(1)}, f32[4,128,64]{1,2,0:T(8,128)}, s32[128]{0:T(128)}, /*index=5*/s32[4096]...) while((s32[]{:T(128)}, f32[4,128]{1,0:T(4,128)S(1)}, ...), condition=%wide.region_21.23_spmd.clone, body=%wide.region_18.22_spmd.clone.sunk | while | flops 476548736 | bytes 14800775 | solution.py:134
  438.8 2.1 constant_dynamic-slice_fusion.19
  447.5 2.1 constant_dynamic-slice_fusion.19
  456.3 2.1 constant_dynamic-slice_fusion.19
  468.8 45.5 %all-reduce.11.cloned.1.call-done = f32[128,1024]{1,0:T(8,128)} async-done(((f32[128,1024]{1,0:T(8,128)}), f32[128,1024]{1,0:T(8,128)}) %all-reduce.11.cloned.1.call-update) | async-done | bytes 524304 | tf_op jit(solution)/shard_map/psum | solution.py:144
  517.3 47.1 %all_to_all.31 = bf16[32,1,20,1024]{3,2,1,0:T(8,128)(2,1)S(1)} all-to-all(bf16[32,1,20,1024]{3,2,1,0:T(8,128)(2,1)S(1)} %bitcast.387), channel_id=1, replica_groups=mesh['section'=2,'tok'=32,'rep'=4] {'tok'}, dimensions={0} | all-to-all | bytes 2621440 | tf_op jit(solution)/shard_map/all_to_all | solution.py:168
  569.0 5.7 all-to-all-start.3
  577.6 33.2 %all-to-all-done.3 = bf16[32,1,20,1024]{3,2,1,0:T(8,128)(2,1)S(1)} async-done(((bf16[32,1,20,1024]{3,2,1,0:T(8,128)(2,1)}), bf16[32,1,20,1024]{3,2,1,0:T(8,128)(2,1)S(1)}, u32[]{:S(2)}, u32[]{:S(2)}) %all-to-all-start.3) | async-done | bytes 1310752 | tf_op jit(solution)/shard_map/all_to_all | solution.py:173
  613.8 2.2 gather_fusion.1
  618.5 46.1 %all-reduce.13.cloned.1.call-done = f32[128,1024]{1,0:T(8,128)} async-done(((f32[128,1024]{1,0:T(8,128)}), f32[128,1024]{1,0:T(8,128)}) %all-reduce.13.cloned.1.call-update) | async-done | bytes 524304 | tf_op jit(solution)/shard_map/psum | solution.py:188
  664.5 2.1 select_bitcast_fusion
  672.4 82.9 %all-gather.8.cloned.1.call-done = bf16[4096,2,256]{0,2,1:T(8,128)(2,1)} async-done(((bf16[128,2,256]{0,2,1:T(8,128)(2,1)}), bf16[4096,2,256]{0,2,1:T(8,128)(2,1)}) %all-gather.8.cloned.1.call-update) | async-done | bytes 4194320 | tf_op jit(solution)/shard_map/all_gather | solution.py:120
  755.3 34.7 %while.56 = (s32[]{:T(128)}, f32[4,128]{1,0:T(4,128)S(1)}, f32[4,128]{1,0:T(4,128)S(1)}, f32[4,128,64]{1,2,0:T(8,128)}, s32[128]{0:T(128)}, /*index=5*/s32[4096]...) while((s32[]{:T(128)}, f32[4,128]{1,0:T(4,128)S(1)}, ...), condition=%wide.region_38.40_spmd.clone, body=%wide.region_35.39_spmd.clone.sunk | while | flops 476548736 | bytes 14800775 | solution.py:134
  793.9 47.8 %all-reduce.15.cloned.1.call-done = f32[128,1024]{1,0:T(8,128)} async-done(((f32[128,1024]{1,0:T(8,128)}), f32[128,1024]{1,0:T(8,128)}) %all-reduce.15.cloned.1.call-update) | async-done | bytes 524304 | tf_op jit(solution)/shard_map/psum | solution.py:144
  846.6 47.1 %all_to_all.32 = bf16[32,1,20,1024]{3,2,1,0:T(8,128)(2,1)S(1)} all-to-all(bf16[32,1,20,1024]{3,2,1,0:T(8,128)(2,1)S(1)} %bitcast.388), channel_id=1, replica_groups=mesh['section'=2,'tok'=32,'rep'=4] {'tok'}, dimensions={0} | all-to-all | bytes 2621440 | tf_op jit(solution)/shard_map/all_to_all | solution.py:168
  898.3 5.9 all-to-all-start.5
  904.6 35.8 %all-to-all-done.5 = bf16[32,1,20,1024]{3,2,1,0:T(8,128)(2,1)} async-done(((bf16[32,1,20,1024]{3,2,1,0:T(8,128)(2,1)}), bf16[32,1,20,1024]{3,2,1,0:T(8,128)(2,1)}, u32[]{:S(2)}, u32[]{:S(2)}) %all-to-all-start.5) | async-done | bytes 1310752 | tf_op jit(solution)/shard_map/all_to_all | solution.py:173
  940.3 3.1 convert_reduce_fusion
  954.1 41.2 %all-reduce.17.cloned.1.call-done = f32[128,1024]{1,0:T(8,128)} async-done(((f32[128,1024]{1,0:T(8,128)}), f32[128,1024]{1,0:T(8,128)}) %all-reduce.17.cloned.1.call-update) | async-done | bytes 524304 | tf_op jit(solution)/shard_map/psum | solution.py:188
  (489 shorter events, 187.3 us)
Async XLA Ops:
  7.2 230.5 %copy-start = (bf16[1,1,1024,2,352]{2,4,3,1,0:T(8,128)(2,1)S(1)}, bf16[1,1,1024,2,352]{2,4,3,1,0:T(8,128)(2,1)}, u32[]{:S(2)}) copy-start(bf16[1,1,1024,2,352]{2,4,3,1,0:T(8,128)(2,1)} %param.26) | copy-start | bytes 4325380
  7.2 93.1 %all-gather.4.cloned.1.call-start = ((), (), s32[]{:S(2)}) async-start(), calls=%async_computation.6 | async-start | bytes 4325376 | tf_op jit(solution)/shard_map/all_gather | solution.py:120
  11.0 89.3 %copy-start.7 = (bf16[1,1024,3,256]{1,3,2,0:T(8,128)(2,1)}, bf16[1,1024,3,256]{1,3,2,0:T(8,128)(2,1)S(1)}, u32[]{:S(2)}) copy-start(bf16[1,1024,3,256]{1,3,2,0:T(8,128)(2,1)S(1)} %copy.83) | copy-start | bytes 4718596
  14.2 172.7 %all-reduce.7.cloned.1.call-start = ((), (), s32[]{:S(2)}) async-start(), calls=%async_computation.7 | async-start | bytes 1048576 | tf_op jit(solution)/shard_map/psum | solution.py:144
  16.2 84.1 %copy-start.45 = (s32[2,128]{1,0:T(2,128)}, s32[2,128]{1,0:T(2,128)S(1)}, u32[]{:S(2)}) copy-start(s32[2,128]{1,0:T(2,128)S(1)} %get-tuple-element.708) | copy-start | bytes 3076
  135.2 51.6 %copy-start.18 = (bf16[2,128,1024]{2,1,0:T(8,128)(2,1)S(1)}, bf16[2,128,1024]{2,1,0:T(8,128)(2,1)}, u32[]{:S(2)}) copy-start(bf16[2,128,1024]{2,1,0:T(8,128)(2,1)} %param.18) | copy-start | bytes 1572868
  242.3 41.9 %all-to-all-start.1 = ((bf16[32,1,20,1024]{3,2,1,0:T(8,128)(2,1)}), bf16[32,1,20,1024]{3,2,1,0:T(8,128)(2,1)S(1)}, u32[]{:S(2)}, u32[]{:S(2)}) async-start(bf16[32,1,20,1024]{3,2,1,0:T(8,128)(2,1)} %copy.87), calls=%async_computation.1 | async-start | bytes 3145728 | tf_op jit(solution)/shard_map/all_to_all | solution.py:173
  248.0 89.7 %all-reduce.9.cloned.1.call-start = ((), (), s32[]{:S(2)}) async-start(), calls=%async_computation.8 | async-start | bytes 1048576 | tf_op jit(solution)/shard_map/psum | solution.py:188
  290.7 51.6 %copy-start.8 = (bf16[1,1024,3,256]{1,3,2,0:T(8,128)(2,1)S(1)}, bf16[1,1024,3,256]{1,3,2,0:T(8,128)(2,1)}, u32[]{:S(2)}) copy-start(bf16[1,1024,3,256]{1,3,2,0:T(8,128)(2,1)} %copy-done.7) | copy-start | bytes 4718596
  290.7 51.6 %copy-start.39 = (f32[1,1,1024]{2,1,0:T(1,128)S(1)}, f32[1,1,1024]{2,1,0:T(1,128)}, u32[]{:S(2)}) copy-start(f32[1,1,1024]{2,1,0:T(1,128)} %copy-done.38) | copy-start | bytes 12292
  291.7 136.0 %all-gather.6.cloned.1.call-start = ((), (), s32[]{:S(2)}) async-start(), calls=%async_computation.9 | async-start | bytes 4325376 | tf_op jit(solution)/shard_map/all_gather | solution.py:120
  339.0 2.4 collective-permute-start
  343.9 170.4 %all-reduce.11.cloned.1.call-start = ((), (), s32[]{:S(2)}) async-start(), calls=%async_computation.10 | async-start | bytes 1048576 | tf_op jit(solution)/shard_map/psum | solution.py:144
  345.2 82.5 %copy-start.31 = (s32[16,2,128]{2,0,1:T(8,128)}, s32[16,2,128]{2,0,1:T(8,128)S(1)}, u32[]{:S(2)}) copy-start(s32[16,2,128]{2,0,1:T(8,128)S(1)} %reduce-window.24) | copy-start | bytes 49156
  462.7 51.6 %copy-start.16 = (bf16[128,1024]{1,0:T(8,128)(2,1)S(1)}, bf16[128,1024]{1,0:T(8,128)(2,1)}, u32[]{:S(2)}) copy-start(bf16[128,1024]{1,0:T(8,128)(2,1)} %copy-done.15) | copy-start | bytes 786436
  569.0 41.9 %all-to-all-start.3 = ((bf16[32,1,20,1024]{3,2,1,0:T(8,128)(2,1)}), bf16[32,1,20,1024]{3,2,1,0:T(8,128)(2,1)S(1)}, u32[]{:S(2)}, u32[]{:S(2)}) async-start(bf16[32,1,20,1024]{3,2,1,0:T(8,128)(2,1)} %copy.93), calls=%async_computation.3 | async-start | bytes 3145728 | tf_op jit(solution)/shard_map/all_to_all | solution.py:173
  574.7 89.8 %all-reduce.13.cloned.1.call-start = ((), (), s32[]{:S(2)}) async-start(), calls=%async_computation.11 | async-start | bytes 1048576 | tf_op jit(solution)/shard_map/psum | solution.py:188
  616.0 48.5 %copy-start.29 = (bf16[128,1024]{1,0:T(8,128)(2,1)S(1)}, bf16[128,1024]{1,0:T(8,128)(2,1)}, u32[]{:S(2)}) copy-start(bf16[128,1024]{1,0:T(8,128)(2,1)} %copy-done.28) | copy-start | bytes 786436
  618.4 51.6 %copy-start.9 = (bf16[1,1024,3,256]{1,3,2,0:T(8,128)(2,1)S(1)}, bf16[1,1024,3,256]{1,3,2,0:T(8,128)(2,1)}, u32[]{:S(2)}) copy-start(bf16[1,1024,3,256]{1,3,2,0:T(8,128)(2,1)} %copy-done.7) | copy-start | bytes 4718596
  618.4 51.6 %copy-start.40 = (f32[1,1,1024]{2,1,0:T(1,128)S(1)}, f32[1,1,1024]{2,1,0:T(1,128)}, u32[]{:S(2)}) copy-start(f32[1,1,1024]{2,1,0:T(1,128)} %copy-done.38) | copy-start | bytes 12292
  618.4 136.9 %all-gather.8.cloned.1.call-start = ((), (), s32[]{:S(2)}) async-start(), calls=%async_computation.12 | async-start | bytes 4325376 | tf_op jit(solution)/shard_map/all_gather | solution.py:120
  666.6 2.4 collective-permute-start.1
  671.5 170.2 %all-reduce.15.cloned.1.call-start = ((), (), s32[]{:S(2)}) async-start(), calls=%async_computation.13 | async-start | bytes 1048576 | tf_op jit(solution)/shard_map/psum | solution.py:144
  790.0 51.6 %copy-start.14 = (bf16[128,1024]{1,0:T(8,128)(2,1)S(1)}, bf16[128,1024]{1,0:T(8,128)(2,1)}, u32[]{:S(2)}) copy-start(bf16[128,1024]{1,0:T(8,128)(2,1)} %copy-done.13) | copy-start | bytes 786436
  898.3 5.9 copy-start.43
  898.3 6.0 copy-start.30
  898.3 6.2 copy-start.46
  898.3 42.0 %all-to-all-start.5 = ((bf16[32,1,20,1024]{3,2,1,0:T(8,128)(2,1)}), bf16[32,1,20,1024]{3,2,1,0:T(8,128)(2,1)}, u32[]{:S(2)}, u32[]{:S(2)}) async-start(bf16[32,1,20,1024]{3,2,1,0:T(8,128)(2,1)} %copy.99), calls=%async_computation.5 | async-start | bytes 3145728 | tf_op jit(solution)/shard_map/all_to_all | solution.py:173
  904.2 91.1 %all-reduce.17.cloned.1.call-start = ((), (), s32[]{:S(2)}) async-start(), calls=%async_computation.14 | async-start | bytes 1048576 | tf_op jit(solution)/shard_map/psum | solution.py:188
  948.3 46.9 %copy-start.20 = (f32[128,1024]{1,0:T(8,128)S(1)}, f32[128,1024]{1,0:T(8,128)}, u32[]{:S(2)}) copy-start(f32[128,1024]{1,0:T(8,128)} %all-reduce.15.cloned.1.call-done) | copy-start | bytes 1572868
  948.3 46.9 %copy-start.26 = (bf16[128,1024]{1,0:T(8,128)(2,1)S(1)}, bf16[128,1024]{1,0:T(8,128)(2,1)}, u32[]{:S(2)}) copy-start(bf16[128,1024]{1,0:T(8,128)(2,1)} %copy-done.25) | copy-start | bytes 786436
  949.2 47.2 %copy-start.27 = (bf16[1,128,1024]{2,1,0:T(8,128)(2,1)S(1)}, bf16[1,128,1024]{2,1,0:T(8,128)(2,1)}, u32[]{:S(2)}) copy-start(bf16[1,128,1024]{2,1,0:T(8,128)(2,1)} %get-tuple-element.669) | copy-start | bytes 786436
  (89 other events, 163.3 us)
Sparse Core Ops, SparseCore 0:
  14.3 85.9 all-gather.3
  138.5 48.3 all-reduce.6
  291.8 45.8 all-reduce.8
  344.0 83.6 all-gather.5
  465.9 48.3 all-reduce.10
  618.5 45.9 all-reduce.12
  671.6 83.6 all-gather.7
  793.3 48.3 all-reduce.14
  949.4 45.8 all-reduce.16
where the time goes:
time: 1010 us; the launch traced here: 1000 us
  waiting for transfers between devices  619 us (61%)
  blocking collectives  141 us (14%)
  other arithmetic  82.9 us (8%)
  local copies, waits for them, and re-layouts  77.7 us (8%)
  matrix products  45.3 us (4%)
  starting transfers between devices  20.6 us (2%)
  between operations  16.4 us (2%)
    all_gather x3, waiting for transfers between devices, per_device(): piece = lax.all_gather(keys_vals, 'tok', axis=0, tiled=True)  242 us
    all_to_all x3, blocking collectives, per_device(): lax.all_to_all(copies, 'tok', split_axis=0, concat_axis=0, tiled=True)  141 us
    psum x3, waiting for transfers between devices, per_device(): mid = resid + lax.psum(attn_part, 'rep')  139 us
    psum x3, waiting for transfers between devices, per_device(): expert_total = lax.psum(expert_local, 'rep')  133 us
    all_to_all x3, waiting for transfers between devices, per_device(): lax.all_to_all(jnp.einsum('secf,efd->secd', hidden, w_down, preferred_ele...  102 us
    slice x12, local copies, waits for them, and re-layouts, attend(): keys_vals[:, 1].reshape(rows_key, heads_here, head_size).astype(jnp.float32)  25.2 us
  transfers between devices with their start and end apart: 14, of which 14 were waited for; matrix products, arithmetic and copies ran while one was open for 3% of the time, Pallas kernels for 0%

commit v1 on v0

--- a/solution.py
+++ b/solution.py
@@ -8,6 +8,22 @@
 PAGE = 128
 CAP = 20
 NEG_FILL = -1e30
+
+
+def body_bind(matrix, named_axis):
+    axis_total = lax.axis_size(named_axis)
+
+    def report_wires(w1, seen_now):
+        if seen_now >= axis_total:
+            return w1
+        value_now = lax.ppermute(
+            w1, named_axis, perm=[(ii, ii ^ seen_now) for ii in range(axis_total)]
+        )
+        y = report_wires(w1 + value_now, 2 * seen_now)
+        return y
+
+    e_now = report_wires(matrix, 1)
+    return e_now
 
 
 def shifted(value, axis, steps):
@@ -185,7 +201,7 @@
         summed = summed.reshape(experts_all * CAP, width)
         gathered = jnp.take(summed, flat_slot, axis=0).reshape(TOP, tok_rows, width)
         expert_local = jnp.sum(gate_vals.T[:, :, None] * gathered, axis=0)
-        expert_total = lax.psum(expert_local, "rep")
+        expert_total = body_bind(expert_local, named_axis="rep")
         layer_result = (mid + expert_total).astype(jnp.bfloat16)
         for slot_micro in range(micro_count):
             if slot_micro == round_index or slot_micro == round_index - 1:

time: 1010 us -> 946 us (0.937)
  waiting for transfers between devices: 619 us -> 536 us
  starting transfers between devices: 20.6 us -> 36.6 us
    psum x3 -> x0, waiting for transfers between devices: 133 us -> none  [per_device(): expert_total = lax.psum(expert_local, 'rep')]
    ppermute x0 -> x6, waiting for transfers between devices: none -> 56.6 us  [report_wires(): lax.ppermute(w1, named_axis, perm=[(ii, ii ^ seen_now) for ii in range(ax...]
    ppermute x0 -> x6, starting transfers between devices: none -> 16.3 us  [report_wires(): lax.ppermute(w1, named_axis, perm=[(ii, ii ^ seen_now) for ii in range(ax...]
  transfers between devices with their start and end apart: 14 -> 17, of which waited for: 14 -> 17; matrix products, arithmetic and copies ran while one was open for 3% -> 3% of each run, Pallas kernels for 0% -> 0%
where the time goes in v1:
time: 946 us; the launch traced here: 935 us
  waiting for transfers between devices  536 us (57%)
  blocking collectives  141 us (15%)
  other arithmetic  79.2 us (8%)
  local copies, waits for them, and re-layouts  77.8 us (8%)
  matrix products  45.3 us (5%)
  starting transfers between devices  36.6 us (4%)
  between operations  17.2 us (2%)
    all_gather x3, waiting for transfers between devices, per_device(): piece = lax.all_gather(keys_vals, 'tok', axis=0, tiled=True)  236 us
    all_to_all x3, blocking collectives, per_device(): lax.all_to_all(copies, 'tok', split_axis=0, concat_axis=0, tiled=True)  141 us
    psum x3, waiting for transfers between devices, per_device(): mid = resid + lax.psum(attn_part, 'rep')  139 us
    all_to_all x3, waiting for transfers between devices, per_device(): lax.all_to_all(jnp.einsum('secf,efd->secd', hidden, w_down, preferred_ele...  102 us
    ppermute x6, waiting for transfers between devices, report_wires(): lax.ppermute(w1, named_axis, perm=[(ii, ii ^ seen_now) for ii in range(ax...  56.6 us
    slice x12, local copies, waits for them, and re-layouts, attend(): keys_vals[:, 1].reshape(rows_key, heads_here, head_size).astype(jnp.float32)  25.2 us
    and x12, other arithmetic, attend(): (seg_query[:, None] == seg_key[None, :]) & (pos_query[:, None] >= pos_key...  19.7 us
  transfers between devices with their start and end apart: 17, of which 17 were waited for; matrix products, arithmetic and copies ran while one was open for 3% of the time, Pallas kernels for 0%

profile of v1, /device:TPU:8, one launch (start us, length us, event | category | flops | bytes accessed | tf_op | source)
XLA Modules:
  0.0 934.6 jit_solution(10413187388867656130)
XLA Ops:
  20.4 79.9 %all-gather.4.cloned.1.call-done = bf16[4096,2,256]{0,2,1:T(8,128)(2,1)} async-done(((bf16[128,2,256]{0,2,1:T(8,128)(2,1)}), bf16[4096,2,256]{0,2,1:T(8,128)(2,1)}) %all-gather.4.cloned.1.call-update) | async-done | bytes 4194320 | tf_op jit(solution)/shard_map/all_gather | solution.py:136
  100.3 34.9 %while.54 = (s32[]{:T(128)}, f32[4,128]{1,0:T(4,128)S(1)}, f32[4,128]{1,0:T(4,128)S(1)}, f32[4,128,64]{1,2,0:T(8,128)}, s32[128]{0:T(128)}, /*index=5*/s32[4096]...) while((s32[]{:T(128)}, f32[4,128]{1,0:T(4,128)S(1)}, ...), condition=%wide.region_4.5_spmd.clone, body=%wide.region_1.4_spmd.clone.sunk | while | flops 476548736 | bytes 14800775 | solution.py:150
  102.7 2.1 constant_dynamic-slice_fusion.18
  140.8 46.1 %all-reduce.4.cloned.1.call-done = f32[128,1024]{1,0:T(8,128)} async-done(((f32[128,1024]{1,0:T(8,128)}), f32[128,1024]{1,0:T(8,128)}) %all-reduce.4.cloned.1.call-update) | async-done | bytes 524304 | tf_op jit(solution)/shard_map/psum | solution.py:160
  190.6 47.1 %all_to_all.30 = bf16[32,1,20,1024]{3,2,1,0:T(8,128)(2,1)S(1)} all-to-all(bf16[32,1,20,1024]{3,2,1,0:T(8,128)(2,1)S(1)} %bitcast.386), channel_id=1, replica_groups=mesh['section'=2,'tok'=32,'rep'=4] {'tok'}, dimensions={0} | all-to-all | bytes 2621440 | tf_op jit(solution)/shard_map/all_to_all | solution.py:184
  242.3 5.7 all-to-all-start.1
  251.2 33.0 %all-to-all-done.1 = bf16[32,1,20,1024]{3,2,1,0:T(8,128)(2,1)S(1)} async-done(((bf16[32,1,20,1024]{3,2,1,0:T(8,128)(2,1)}), bf16[32,1,20,1024]{3,2,1,0:T(8,128)(2,1)S(1)}, u32[]{:S(2)}, u32[]{:S(2)}) %all-to-all-start.1) | async-done | bytes 1310752 | tf_op jit(solution)/shard_map/all_to_all | solution.py:189
  287.2 2.2 gather_fusion
  292.5 10.6 %collective-permute-done = f32[128,1024]{1,0:T(8,128)S(1)} collective-permute-done((f32[128,1024]{1,0:T(8,128)S(1)}, f32[128,1024]{1,0:T(8,128)S(1)}, u32[]{:S(2)}, u32[]{:S(2)}) %collective-permute-start) | collective-permute-done | bytes 524320 | tf_op jit(solution)/shard_map/ppermute | solution.py:19
  303.2 3.9 collective-permute-start.1
  307.1 9.8 %collective-permute-done.1 = f32[128,1024]{1,0:T(8,128)S(1)} collective-permute-done((f32[128,1024]{1,0:T(8,128)S(1)}, f32[128,1024]{1,0:T(8,128)S(1)}, u32[]{:S(2)}, u32[]{:S(2)}) %collective-permute-start.1) | collective-permute-done | bytes 524320 | tf_op jit(solution)/shard_map/ppermute | solution.py:19
  325.4 76.7 %all-gather.6.cloned.1.call-done = bf16[4096,2,256]{0,2,1:T(8,128)(2,1)} async-done(((bf16[128,2,256]{0,2,1:T(8,128)(2,1)}), bf16[4096,2,256]{0,2,1:T(8,128)(2,1)}) %all-gather.6.cloned.1.call-update) | async-done | bytes 4194320 | tf_op jit(solution)/shard_map/all_gather | solution.py:136
  402.1 35.0 %while.55 = (s32[]{:T(128)}, f32[4,128]{1,0:T(4,128)S(1)}, f32[4,128]{1,0:T(4,128)S(1)}, f32[4,128,64]{1,2,0:T(8,128)}, s32[128]{0:T(128)}, /*index=5*/s32[4096]...) while((s32[]{:T(128)}, f32[4,128]{1,0:T(4,128)S(1)}, ...), condition=%wide.region_20.22_spmd.clone, body=%wide.region_17.21_spmd.clone.sunk | while | flops 476548736 | bytes 14800775 | solution.py:150
  443.2 45.5 %all-reduce.6.cloned.1.call-done = f32[128,1024]{1,0:T(8,128)} async-done(((f32[128,1024]{1,0:T(8,128)}), f32[128,1024]{1,0:T(8,128)}) %all-reduce.6.cloned.1.call-update) | async-done | bytes 524304 | tf_op jit(solution)/shard_map/psum | solution.py:160
  491.7 47.1 %all_to_all.31 = bf16[32,1,20,1024]{3,2,1,0:T(8,128)(2,1)S(1)} all-to-all(bf16[32,1,20,1024]{3,2,1,0:T(8,128)(2,1)S(1)} %bitcast.387), channel_id=1, replica_groups=mesh['section'=2,'tok'=32,'rep'=4] {'tok'}, dimensions={0} | all-to-all | bytes 2621440 | tf_op jit(solution)/shard_map/all_to_all | solution.py:184
  543.4 5.7 all-to-all-start.3
  552.0 33.2 %all-to-all-done.3 = bf16[32,1,20,1024]{3,2,1,0:T(8,128)(2,1)S(1)} async-done(((bf16[32,1,20,1024]{3,2,1,0:T(8,128)(2,1)}), bf16[32,1,20,1024]{3,2,1,0:T(8,128)(2,1)S(1)}, u32[]{:S(2)}, u32[]{:S(2)}) %all-to-all-start.3) | async-done | bytes 1310752 | tf_op jit(solution)/shard_map/all_to_all | solution.py:189
  588.2 2.2 gather_fusion.1
  593.6 10.6 %collective-permute-done.3 = f32[128,1024]{1,0:T(8,128)S(1)} collective-permute-done((f32[128,1024]{1,0:T(8,128)S(1)}, f32[128,1024]{1,0:T(8,128)S(1)}, u32[]{:S(2)}, u32[]{:S(2)}) %collective-permute-start.3) | collective-permute-done | bytes 524320 | tf_op jit(solution)/shard_map/ppermute | solution.py:19
  605.1 3.8 collective-permute-start.4
  608.9 10.1 %collective-permute-done.4 = f32[128,1024]{1,0:T(8,128)} collective-permute-done((f32[128,1024]{1,0:T(8,128)}, f32[128,1024]{1,0:T(8,128)}, u32[]{:S(2)}, u32[]{:S(2)}) %collective-permute-start.4) | collective-permute-done | bytes 524320 | tf_op jit(solution)/shard_map/ppermute | solution.py:19
  619.0 2.3 select_bitcast_fusion
  626.8 79.4 %all-gather.8.cloned.1.call-done = bf16[4096,2,256]{0,2,1:T(8,128)(2,1)} async-done(((bf16[128,2,256]{0,2,1:T(8,128)(2,1)}), bf16[4096,2,256]{0,2,1:T(8,128)(2,1)}) %all-gather.8.cloned.1.call-update) | async-done | bytes 4194320 | tf_op jit(solution)/shard_map/all_gather | solution.py:136
  706.2 34.7 %while.56 = (s32[]{:T(128)}, f32[4,128]{1,0:T(4,128)S(1)}, f32[4,128]{1,0:T(4,128)S(1)}, f32[4,128,64]{1,2,0:T(8,128)}, s32[128]{0:T(128)}, /*index=5*/s32[4096]...) while((s32[]{:T(128)}, f32[4,128]{1,0:T(4,128)S(1)}, ...), condition=%wide.region_36.38_spmd.clone, body=%wide.region_33.37_spmd.clone.sunk | while | flops 476548736 | bytes 14800775 | solution.py:150
  744.8 47.8 %all-reduce.8.cloned.1.call-done = f32[128,1024]{1,0:T(8,128)} async-done(((f32[128,1024]{1,0:T(8,128)}), f32[128,1024]{1,0:T(8,128)}) %all-reduce.8.cloned.1.call-update) | async-done | bytes 524304 | tf_op jit(solution)/shard_map/psum | solution.py:160
  797.5 47.1 %all_to_all.32 = bf16[32,1,20,1024]{3,2,1,0:T(8,128)(2,1)S(1)} all-to-all(bf16[32,1,20,1024]{3,2,1,0:T(8,128)(2,1)S(1)} %bitcast.388), channel_id=1, replica_groups=mesh['section'=2,'tok'=32,'rep'=4] {'tok'}, dimensions={0} | all-to-all | bytes 2621440 | tf_op jit(solution)/shard_map/all_to_all | solution.py:184
  849.2 5.9 all-to-all-start.5
  855.4 35.8 %all-to-all-done.5 = bf16[32,1,20,1024]{3,2,1,0:T(8,128)(2,1)} async-done(((bf16[32,1,20,1024]{3,2,1,0:T(8,128)(2,1)}), bf16[32,1,20,1024]{3,2,1,0:T(8,128)(2,1)}, u32[]{:S(2)}, u32[]{:S(2)}) %all-to-all-start.5) | async-done | bytes 1310752 | tf_op jit(solution)/shard_map/all_to_all | solution.py:189
  891.2 3.1 convert_reduce_fusion
  901.0 10.6 %collective-permute-done.6 = f32[128,1024]{1,0:T(8,128)S(1)} collective-permute-done((f32[128,1024]{1,0:T(8,128)S(1)}, f32[128,1024]{1,0:T(8,128)S(1)}, u32[]{:S(2)}, u32[]{:S(2)}) %collective-permute-start.6) | collective-permute-done | bytes 524320 | tf_op jit(solution)/shard_map/ppermute | solution.py:19
  911.7 3.7 collective-permute-start.7
  920.3 5.0 collective-permute-done.7
  (501 shorter events, 200.8 us)
Async XLA Ops:
  7.2 230.5 %copy-start = (bf16[1,1,1024,2,352]{2,4,3,1,0:T(8,128)(2,1)S(1)}, bf16[1,1,1024,2,352]{2,4,3,1,0:T(8,128)(2,1)}, u32[]{:S(2)}) copy-start(bf16[1,1,1024,2,352]{2,4,3,1,0:T(8,128)(2,1)} %param.26) | copy-start | bytes 4325380
  7.2 93.1 %all-gather.4.cloned.1.call-start = ((), (), s32[]{:S(2)}) async-start(), calls=%async_computation.6 | async-start | bytes 4325376 | tf_op jit(solution)/shard_map/all_gather | solution.py:136
  11.0 89.3 %copy-start.7 = (bf16[1,1024,3,256]{1,3,2,0:T(8,128)(2,1)}, bf16[1,1024,3,256]{1,3,2,0:T(8,128)(2,1)S(1)}, u32[]{:S(2)}) copy-start(bf16[1,1024,3,256]{1,3,2,0:T(8,128)(2,1)S(1)} %copy.83) | copy-start | bytes 4718596
  14.2 172.7 %all-reduce.4.cloned.1.call-start = ((), (), s32[]{:S(2)}) async-start(), calls=%async_computation.7 | async-start | bytes 1048576 | tf_op jit(solution)/shard_map/psum | solution.py:160
  16.2 84.1 %copy-start.48 = (s32[2,128]{1,0:T(2,128)}, s32[2,128]{1,0:T(2,128)S(1)}, u32[]{:S(2)}) copy-start(s32[2,128]{1,0:T(2,128)S(1)} %get-tuple-element.708) | copy-start | bytes 3076
  135.2 51.6 %copy-start.18 = (bf16[2,128,1024]{2,1,0:T(8,128)(2,1)S(1)}, bf16[2,128,1024]{2,1,0:T(8,128)(2,1)}, u32[]{:S(2)}) copy-start(bf16[2,128,1024]{2,1,0:T(8,128)(2,1)} %param.18) | copy-start | bytes 1572868
  242.3 41.9 %all-to-all-start.1 = ((bf16[32,1,20,1024]{3,2,1,0:T(8,128)(2,1)}), bf16[32,1,20,1024]{3,2,1,0:T(8,128)(2,1)S(1)}, u32[]{:S(2)}, u32[]{:S(2)}) async-start(bf16[32,1,20,1024]{3,2,1,0:T(8,128)(2,1)} %copy.87), calls=%async_computation.1 | async-start | bytes 3145728 | tf_op jit(solution)/shard_map/all_to_all | solution.py:189
  248.0 154.1 %all-gather.6.cloned.1.call-start = ((), (), s32[]{:S(2)}) async-start(), calls=%async_computation.8 | async-start | bytes 4325376 | tf_op jit(solution)/shard_map/all_gather | solution.py:136
  290.7 26.1 %copy-start.20 = (f32[128,1024]{1,0:T(8,128)S(1)}, f32[128,1024]{1,0:T(8,128)}, u32[]{:S(2)}) copy-start(f32[128,1024]{1,0:T(8,128)} %all-reduce.4.cloned.1.call-done) | copy-start | bytes 1572868
  290.9 29.6 %copy-start.8 = (bf16[1,1024,3,256]{1,3,2,0:T(8,128)(2,1)S(1)}, bf16[1,1024,3,256]{1,3,2,0:T(8,128)(2,1)}, u32[]{:S(2)}) copy-start(bf16[1,1024,3,256]{1,3,2,0:T(8,128)(2,1)} %copy-done.7) | copy-start | bytes 4718596
  290.9 29.6 %copy-start.40 = (f32[1,1,1024]{2,1,0:T(1,128)S(1)}, f32[1,1,1024]{2,1,0:T(1,128)}, u32[]{:S(2)}) copy-start(f32[1,1,1024]{2,1,0:T(1,128)} %copy-done.39) | copy-start | bytes 12292
  290.9 12.3 %collective-permute-start = (f32[128,1024]{1,0:T(8,128)S(1)}, f32[128,1024]{1,0:T(8,128)S(1)}, u32[]{:S(2)}, u32[]{:S(2)}) collective-permute-start(f32[128,1024]{1,0:T(8,128)S(1)} %multiply_reduce_fusion.2), channel_id=1, source_target_pairs={{0,1},{1,0},{2,3},{3,2},{4,5},{5,4},{6,7},{7,6},{8,9},{9,8},{10,11... | collective-permute-start | bytes 1572872 | tf_op jit(solution)/shard_map/ppermute | solution.py:19
  303.2 13.6 %collective-permute-start.1 = (f32[128,1024]{1,0:T(8,128)S(1)}, f32[128,1024]{1,0:T(8,128)S(1)}, u32[]{:S(2)}, u32[]{:S(2)}) collective-permute-start(f32[128,1024]{1,0:T(8,128)S(1)} %add.387), channel_id=1, source_target_pairs={{0,2},{1,3},{2,0},{3,1},{4,6},{5,7},{6,4},{7,5},{8,10},{9,11},{10,... | collective-permute-start | bytes 1572872 | tf_op jit(solution)/shard_map/ppermute | solution.py:19
  317.0 2.6 collective-permute-start.2
  322.0 166.7 %all-reduce.6.cloned.1.call-start = ((), (), s32[]{:S(2)}) async-start(), calls=%async_computation.9 | async-start | bytes 1048576 | tf_op jit(solution)/shard_map/psum | solution.py:160
  322.7 79.4 %copy-start.32 = (s32[16,2,128]{2,0,1:T(8,128)}, s32[16,2,128]{2,0,1:T(8,128)S(1)}, u32[]{:S(2)}) copy-start(s32[16,2,128]{2,0,1:T(8,128)S(1)} %reduce-window.24) | copy-start | bytes 49156
  437.1 51.6 %copy-start.16 = (bf16[128,1024]{1,0:T(8,128)(2,1)S(1)}, bf16[128,1024]{1,0:T(8,128)(2,1)}, u32[]{:S(2)}) copy-start(bf16[128,1024]{1,0:T(8,128)(2,1)} %copy-done.15) | copy-start | bytes 786436
  543.4 41.9 %all-to-all-start.3 = ((bf16[32,1,20,1024]{3,2,1,0:T(8,128)(2,1)}), bf16[32,1,20,1024]{3,2,1,0:T(8,128)(2,1)S(1)}, u32[]{:S(2)}, u32[]{:S(2)}) async-start(bf16[32,1,20,1024]{3,2,1,0:T(8,128)(2,1)} %copy.93), calls=%async_computation.3 | async-start | bytes 3145728 | tf_op jit(solution)/shard_map/all_to_all | solution.py:189
  549.1 157.1 %all-gather.8.cloned.1.call-start = ((), (), s32[]{:S(2)}) async-start(), calls=%async_computation.10 | async-start | bytes 4325376 | tf_op jit(solution)/shard_map/all_gather | solution.py:136
  591.8 27.2 %copy-start.29 = (bf16[128,1024]{1,0:T(8,128)(2,1)S(1)}, bf16[128,1024]{1,0:T(8,128)(2,1)}, u32[]{:S(2)}) copy-start(bf16[128,1024]{1,0:T(8,128)(2,1)} %copy-done.28) | copy-start | bytes 786436
  591.9 12.3 %collective-permute-start.3 = (f32[128,1024]{1,0:T(8,128)S(1)}, f32[128,1024]{1,0:T(8,128)S(1)}, u32[]{:S(2)}, u32[]{:S(2)}) collective-permute-start(f32[128,1024]{1,0:T(8,128)S(1)} %multiply_reduce_fusion.1), channel_id=1, source_target_pairs={{0,1},{1,0},{2,3},{3,2},{4,5},{5,4},{6,7},{7,6},{8,9},{9,8},{10,11... | collective-permute-start | bytes 1572872 | tf_op jit(solution)/shard_map/ppermute | solution.py:19
  605.1 19.5 %copy-start.9 = (bf16[1,1024,3,256]{1,3,2,0:T(8,128)(2,1)S(1)}, bf16[1,1024,3,256]{1,3,2,0:T(8,128)(2,1)}, u32[]{:S(2)}) copy-start(bf16[1,1024,3,256]{1,3,2,0:T(8,128)(2,1)} %copy-done.7) | copy-start | bytes 4718596
  605.1 19.5 %copy-start.41 = (f32[1,1,1024]{2,1,0:T(1,128)S(1)}, f32[1,1,1024]{2,1,0:T(1,128)}, u32[]{:S(2)}) copy-start(f32[1,1,1024]{2,1,0:T(1,128)} %copy-done.39) | copy-start | bytes 12292
  605.1 13.9 %collective-permute-start.4 = (f32[128,1024]{1,0:T(8,128)}, f32[128,1024]{1,0:T(8,128)}, u32[]{:S(2)}, u32[]{:S(2)}) collective-permute-start(f32[128,1024]{1,0:T(8,128)} %add.397), channel_id=1, source_target_pairs={{0,2},{1,3},{2,0},{3,1},{4,6},{5,7},{6,4},{7,5},{8,10},{9,11},{10,... | collective-permute-start | bytes 1572872 | tf_op jit(solution)/shard_map/ppermute | solution.py:19
  621.2 2.4 collective-permute-start.5
  626.1 166.5 %all-reduce.8.cloned.1.call-start = ((), (), s32[]{:S(2)}) async-start(), calls=%async_computation.11 | async-start | bytes 1048576 | tf_op jit(solution)/shard_map/psum | solution.py:160
  740.9 51.6 %copy-start.14 = (bf16[128,1024]{1,0:T(8,128)(2,1)S(1)}, bf16[128,1024]{1,0:T(8,128)(2,1)}, u32[]{:S(2)}) copy-start(bf16[128,1024]{1,0:T(8,128)(2,1)} %copy-done.13) | copy-start | bytes 786436
  849.2 42.0 %all-to-all-start.5 = ((bf16[32,1,20,1024]{3,2,1,0:T(8,128)(2,1)}), bf16[32,1,20,1024]{3,2,1,0:T(8,128)(2,1)}, u32[]{:S(2)}, u32[]{:S(2)}) async-start(bf16[32,1,20,1024]{3,2,1,0:T(8,128)(2,1)} %copy.99), calls=%async_computation.5 | async-start | bytes 3145728 | tf_op jit(solution)/shard_map/all_to_all | solution.py:189
  899.2 26.1 %copy-start.21 = (f32[128,1024]{1,0:T(8,128)S(1)}, f32[128,1024]{1,0:T(8,128)}, u32[]{:S(2)}) copy-start(f32[128,1024]{1,0:T(8,128)} %all-reduce.8.cloned.1.call-done) | copy-start | bytes 1572868
  899.2 26.1 %copy-start.27 = (bf16[128,1024]{1,0:T(8,128)(2,1)S(1)}, bf16[128,1024]{1,0:T(8,128)(2,1)}, u32[]{:S(2)}) copy-start(bf16[128,1024]{1,0:T(8,128)(2,1)} %copy-done.26) | copy-start | bytes 786436
  899.3 12.2 %collective-permute-start.6 = (f32[128,1024]{1,0:T(8,128)S(1)}, f32[128,1024]{1,0:T(8,128)S(1)}, u32[]{:S(2)}, u32[]{:S(2)}) collective-permute-start(f32[128,1024]{1,0:T(8,128)S(1)} %multiply_reduce_fusion), channel_id=1, source_target_pairs={{0,1},{1,0},{2,3},{3,2},{4,5},{5,4},{6,7},{7,6},{8,9},{9,8},{10,11... | collective-permute-start | bytes 1572872 | tf_op jit(solution)/shard_map/ppermute | solution.py:19
  911.7 13.6 %collective-permute-start.7 = (f32[128,1024]{1,0:T(8,128)S(1)}, f32[128,1024]{1,0:T(8,128)}, u32[]{:S(2)}, u32[]{:S(2)}) collective-permute-start(f32[128,1024]{1,0:T(8,128)S(1)} %add.407), channel_id=1, source_target_pairs={{0,2},{1,3},{2,0},{3,1},{4,6},{5,7},{6,4},{7,5},{8,10},{9,11},{10,... | collective-permute-start | bytes 1572872 | tf_op jit(solution)/shard_map/ppermute | solution.py:19
  (95 other events, 230.6 us)
Sparse Core Ops, SparseCore 0:
  14.3 85.9 all-gather.3
  138.5 48.3 all-reduce.3
  322.2 79.9 all-gather.5
  440.3 48.3 all-reduce.5
  626.2 79.9 all-gather.7
  744.2 48.3 all-reduce.7
